TPU v7x, 256 devices: a whole 4x4x8 slice. The times are simulated.
256 devices in a mesh: row: 64 (over z, y, core), col: 4 (over x).
Axes of the slice: x: 4, y: 4, z: 8, core: 2. Of those that a mesh axis runs over, the one named last changes fastest.
Arguments:
- panel_adj: float32 [24576, 512], P('row', 'col'), may hold values from -16 to 16
- inv_tile: float32 [512, 512], P('col'), may hold values from -1 to 2, as said below
- factor_panel: float32 [24576, 512], P('row', 'col'), may hold values from -0.0390625 to 0.0390625
- block_row: float32 [512, 8192], P('row', 'col'), may hold values from -0.25 to 0.25
- slab: float32 [24576, 8192], P('row', 'col'), may hold values from -0.0390625 to 0.0390625
- slab_adj: float32 [24576, 8192], P('row', 'col'), may hold values from -6 to 6
- row_adj: float32 [512, 8192], P('row', 'col'), may hold values from -6 to 6
- diag_adj: float32 [512, 512], P('row', 'col'), may hold values from -6 to 6
Outputs:
- panel_out: float32 [24576, 512], P('row', 'col')
- slab_out: float32 [24576, 8192], P('row', 'col')
- row_out: float32 [512, 8192], P('row', 'col')
- diag_out: float32 [512, 512], P('row', 'col')
Inputs may be any that keep to these rules, and one draw needn't show every extreme that they name: inv_tile is lower triangular with diagonal entries between 1 and 2.
All inputs are finite; a program needn't handle non-finite values.
Results may differ from a plain program's by a relative error of at most 0.00011.
Values sent between devices are 32-bit elements; how exact they have to be, the bound alone decides.
No kernel may reach another device: no remote copies, remote signals or barrier semaphores. Data moves between devices by JAX's collectives and lax.ppermute only.
A program may use at most 64 MiB of HBM per device.

v0:
```python
import jax
import jax.numpy as jnp
from jax import lax
from jax.sharding import PartitionSpec as P


def contract_rows(left, right):
    return lax.dot_general(
        left,
        right,
        (((0,), (0,)), ((), ())),
        precision=lax.Precision.HIGHEST,
        preferred_element_type=jnp.float32,
    )


def per_device(panel_adj, inv_tile, factor_panel, block_row, slab, slab_adj, row_adj, diag_adj):
    precise = lax.Precision.HIGHEST
    col_width = panel_adj.shape[1]
    col_place = lax.axis_index("col")
    share = diag_adj.shape[0]
    partial_panel = jnp.dot(
        panel_adj, inv_tile, precision=precise, preferred_element_type=jnp.float32
    )
    scaled = lax.psum(partial_panel, "col")
    panel_out = lax.dynamic_slice_in_dim(scaled, col_place * col_width, col_width, 1)
    slab_out = slab_adj - jnp.dot(
        scaled,
        lax.all_gather(block_row, "row", axis=0, tiled=True),
        precision=precise,
        preferred_element_type=jnp.float32,
    )
    row_term = lax.psum_scatter(contract_rows(scaled, slab), "row", scatter_dimension=0, tiled=True)
    diag_term = lax.psum_scatter(
        contract_rows(scaled, factor_panel), "row", scatter_dimension=0, tiled=True
    )
    row_ids = lax.broadcasted_iota(jnp.int32, diag_adj.shape, 0) + lax.axis_index("row") * share
    col_ids = lax.broadcasted_iota(jnp.int32, diag_adj.shape, 1) + col_place * col_width
    diag_out = diag_adj - jnp.where(col_ids <= row_ids, diag_term, 0.0)
    return (panel_out, slab_out, row_adj - row_term, diag_out)


def solution(mesh):
    return jax.shard_map(
        per_device,
        mesh=mesh,
        in_specs=(
            P("row", "col"),
            P("col", None),
            P("row", "col"),
            P("row", "col"),
            P("row", "col"),
            P("row", "col"),
            P("row", "col"),
            P("row", "col"),
        ),
        out_specs=(P("row", "col"), P("row", "col"), P("row", "col"), P("row", "col")),
        check_vma=False,
    )
```

profile of v0, /device:TPU:1, one launch (start us, length us, event | category | flops | bytes accessed | tf_op | source)
XLA Modules:
  0.0 371.2 jit_solution(2602399601953829121)
XLA Ops:
  7.2 0.0 copy-start
  7.2 0.0 all-reduce.6.cloned.1.call-start
  7.2 2.8 fusion.1
  10.1 0.0 all-reduce.6.cloned.1.call-update
  10.1 0.0 copy-start.2
  10.1 0.0 all-reduce.8.cloned.1.call-start
  10.2 52.2 %all-reduce.6.cloned.1.call-done = f32[384,512]{1,0:T(8,128)} async-done(((f32[384,512]{1,0:T(8,128)}), f32[384,512]{1,0:T(8,128)}) %all-reduce.6.cloned.1.call-update) | async-done | bytes 786448 | tf_op jit(solution)/shard_map/psum | solution.py:25
  62.4 0.0 copy-done
  62.4 9.5 %fusion.2 = f32[512,2048]{1,0:T(8,128)} fusion(f32[384,512]{1,0:T(8,128)} %all-reduce.6.cloned.1.call-done, f32[384,2048]{1,0:T(8,128)S(1)} %copy-done), kind=kOutput, calls=%fused_computation.8 | convolution fusion | flops 4831838208 | bytes 8126464 | tf_op jit(solution)/shard_map/dot_general | solution.py:8
  71.8 0.0 copy-done.2
  71.8 0.0 copy-done.1
  71.9 0.0 copy-start.4
  71.9 0.0 copy-start.3
  71.9 2.2 fusion.3
  74.1 0.0 all-reduce.8.cloned.1.call-update
  74.1 0.0 all-gather.2.cloned.1.call-start
  74.2 0.7 all-gather.2.cloned.1.call-update
  74.9 0.6 dynamic-slice
  76.1 1.6 constant_dynamic-slice_fusion
  77.8 194.3 %all-reduce.8.cloned.1.call-done = (f32[512,2048]{1,0:T(8,128)}, f32[512,128]{1,0:T(8,128)}) async-done(((f32[512,2048]{1,0:T(8,128)}, f32[512,128]{1,0:T(8,128)}), (f32[512,2048]{1,0:T(8,128)}, f32[512,128]{1,0:T(8,128)})) %all-reduce.8.cloned.1.call-update) | async-done | bytes 4456464
  272.1 1.3 fusion
  273.4 1.5 dynamic-slice_subtract_fusion
  274.9 80.2 %all-gather.2.cloned.1.call-done = f32[512,2048]{1,0:T(8,128)} async-done(((f32[8,2048]{1,0:T(8,128)}), f32[512,2048]{1,0:T(8,128)}) %all-gather.2.cloned.1.call-update) | async-done | bytes 4194320 | tf_op jit(solution)/shard_map/all_gather | solution.py:29
  355.1 9.6 %convolution_subtract_fusion = f32[384,2048]{1,0:T(8,128)} fusion(f32[384,2048]{1,0:T(8,128)} %param.13, f32[384,512]{1,0:T(8,128)} %all-reduce.6.cloned.1.call-done, f32[512,2048]{1,0:T(8,128)} %all-gather.2.cloned.1.call-done), kind=kOutput, calls=%fused_computation | convolution fusion | flops 4832624640 | bytes 11272192 | tf_op jit(solution)/shard_map/dot_general | solution.py:27
  (7 shorter events, 0.0 us)
Async XLA Ops:
  7.2 55.2 %copy-start = (f32[384,2048]{1,0:T(8,128)S(1)}, f32[384,2048]{1,0:T(8,128)}, u32[]{:S(2)}) copy-start(f32[384,2048]{1,0:T(8,128)} %param.12) | copy-start | bytes 9437188
  7.2 55.2 %all-reduce.6.cloned.1.call-start = ((), (), s32[]{:S(2)}) async-start(), calls=%async_computation | async-start | bytes 1572864 | tf_op jit(solution)/shard_map/psum | solution.py:25
  10.1 61.7 %copy-start.2 = (f32[384,128]{1,0:T(8,128)S(1)}, f32[384,128]{1,0:T(8,128)}, u32[]{:S(2)}) copy-start(f32[384,128]{1,0:T(8,128)} %param.10) | copy-start | bytes 589828
  10.1 262.0 %all-reduce.8.cloned.1.call-start = ((), (), s32[]{:S(2)}) async-start(), calls=%async_computation.2 | async-start | bytes 8912896
  62.4 9.5 %copy-start.1 = (f32[384,512]{1,0:T(8,128)S(1)}, f32[384,512]{1,0:T(8,128)}, u32[]{:S(2)}) copy-start(f32[384,512]{1,0:T(8,128)} %all-reduce.6.cloned.1.call-done) | copy-start | bytes 2359300
  71.8 3.0 copy-start.5
  71.9 200.2 %copy-start.4 = (f32[8,128]{1,0:T(8,128)S(1)}, f32[8,128]{1,0:T(8,128)}, u32[]{:S(2)}) copy-start(f32[8,128]{1,0:T(8,128)} %param.15) | copy-start | bytes 12292
  71.9 201.6 %copy-start.3 = (f32[8,2048]{1,0:T(8,128)S(1)}, f32[8,2048]{1,0:T(8,128)}, u32[]{:S(2)}) copy-start(f32[8,2048]{1,0:T(8,128)} %param.14) | copy-start | bytes 196612
  74.1 280.9 %all-gather.2.cloned.1.call-start = ((), (), s32[]{:S(2)}) async-start(), calls=%async_computation.1 | async-start | bytes 4259840 | tf_op jit(solution)/shard_map/all_gather | solution.py:29
Sparse Core Ops, SparseCore 0:
  10.9 51.3 all-reduce.5
  74.2 197.7 all-reduce.7
  274.9 80.1 all-gather.1
where the time goes:
time: 371 us
  waiting for transfers between devices  327 us (88%)
  matrix products  24.1 us (6%)
  between operations  14.5 us (4%)
    unnamed x4, waiting for transfers between devices  195 us
    all_gather x1, waiting for transfers between devices, per_device(): lax.all_gather(block_row, 'row', axis=0, tiled=True)  80.2 us
    psum x1, waiting for transfers between devices, per_device(): scaled = lax.psum(partial_panel, 'col')  52.2 us
    dot_general x2, matrix products, contract_rows(): lax.dot_general(left, right, (((0,), (0,)), ((), ())), precision=lax.Prec...  11.7 us
    dot_general x1, matrix products, per_device(): jnp.dot(scaled, lax.all_gather(block_row, 'row', axis=0, tiled=True), pre...  9.61 us
  transfers between devices with their start and end apart: 3, of which 3 were waited for; matrix products, arithmetic and copies ran while one was open for 1% of the time, Pallas kernels for 0%

commit v1 on v0

--- a/solution.py
+++ b/solution.py
@@ -26,7 +26,9 @@
     panel_out = lax.dynamic_slice_in_dim(scaled, col_place * col_width, col_width, 1)
     slab_out = slab_adj - jnp.dot(
         scaled,
-        lax.all_gather(block_row, "row", axis=0, tiled=True),
+        jnp.concatenate(
+            lax.all_to_all(jnp.stack([block_row] * lax.axis_size("row")), "row", 0, 0), axis=0
+        ),
         precision=precise,
         preferred_element_type=jnp.float32,
     )

time: 371 us -> 313 us (0.84)
  waiting for transfers between devices: 327 us -> 250 us
  starting transfers between devices: 0.12 us -> 13.5 us
  local copies, waits for them, and re-layouts: 2.25 us -> 6.34 us
    all_gather x1 -> x0, waiting for transfers between devices: 80.2 us -> none  [per_device(): lax.all_gather(block_row, 'row', axis=0, tiled=True)]
    all_to_all x0 -> x1, starting transfers between devices: none -> 13.5 us  [per_device(): lax.all_to_all(jnp.stack([block_row] * lax.axis_size('row')), 'row', 0, 0)]
    unnamed x4 -> x3, waiting for transfers between devices: 195 us -> 199 us
  transfers between devices with their start and end apart: 3 -> 3, of which waited for: 3 -> 2; matrix products, arithmetic and copies ran while one was open for 1% -> 7% of each run, Pallas kernels for 0% -> 0%
where the time goes in v1:
time: 313 us; the launch traced here: 312 us
  waiting for transfers between devices  250 us (80%)
  matrix products  24.9 us (8%)
  between operations  14.7 us (5%)
  starting transfers between devices  13.5 us (4%)
  local copies, waits for them, and re-layouts  6.34 us (2%)
    unnamed x3, waiting for transfers between devices  199 us
    psum x1, waiting for transfers between devices, per_device(): scaled = lax.psum(partial_panel, 'col')  50.4 us
    all_to_all x1, starting transfers between devices, per_device(): lax.all_to_all(jnp.stack([block_row] * lax.axis_size('row')), 'row', 0, 0)  13.5 us
    dot_general x2, matrix products, contract_rows(): lax.dot_general(left, right, (((0,), (0,)), ((), ())), precision=lax.Prec...  12.7 us
    dot_general x1, matrix products, per_device(): jnp.dot(scaled, jnp.concatenate(lax.all_to_all(jnp.stack([block_row] * la...  9.61 us
  transfers between devices with their start and end apart: 3, of which 2 were waited for; matrix products, arithmetic and copies ran while one was open for 7% of the time, Pallas kernels for 0%

profile of v1, /device:TPU:1, one launch (start us, length us, event | category | flops | bytes accessed | tf_op | source)
XLA Modules:
  0.0 312.1 jit_solution(11668526658773828954)
XLA Ops:
  7.2 0.0 copy-start
  7.2 3.5 %stack.2 = f32[64,8,2048]{2,1,0:T(8,128)} broadcast(f32[8,2048]{1,0:T(8,128)} %param.11), dimensions={1,2} | broadcast | bytes 4259840 | tf_op jit(solution)/shard_map/stack | solution.py:30
  10.7 0.0 copy-start.1
  10.7 13.5 %all-to-all-start = ((f32[64,8,2048]{2,1,0:T(8,128)}), f32[64,8,2048]{2,1,0:T(8,128)}, u32[]{:S(2)}, u32[]{:S(2)}) async-start(f32[64,8,2048]{2,1,0:T(8,128)} %stack.2), calls=%async_computation | async-start | bytes 8388608 | tf_op jit(solution)/shard_map/all_to_all | solution.py:30
  24.1 0.0 all-reduce.6.cloned.1.call-start
  24.2 0.0 copy-done.1
  24.2 2.6 fusion.6
  26.8 0.0 all-reduce.6.cloned.1.call-update
  26.8 0.0 all-reduce.8.cloned.1.call-start
  26.8 50.4 %all-reduce.6.cloned.1.call-done = f32[384,512]{1,0:T(8,128)} async-done(((f32[384,512]{1,0:T(8,128)}), f32[384,512]{1,0:T(8,128)}) %all-reduce.6.cloned.1.call-update) | async-done | bytes 786448 | tf_op jit(solution)/shard_map/psum | solution.py:25
  77.3 3.3 %fusion.8 = f32[512,128]{1,0:T(8,128)} fusion(f32[384,512]{1,0:T(8,128)} %all-reduce.6.cloned.1.call-done, f32[384,128]{1,0:T(8,128)} %param.10), kind=kOutput, calls=%fused_computation.11 | convolution fusion | flops 301989888 | bytes 1245184 | tf_op jit(solution)/shard_map/dot_general | solution.py:8
  80.6 0.0 copy-done
  80.6 9.4 %fusion.7 = f32[512,2048]{1,0:T(8,128)} fusion(f32[384,512]{1,0:T(8,128)} %all-reduce.6.cloned.1.call-done, f32[384,2048]{1,0:T(8,128)S(1)} %copy-done), kind=kOutput, calls=%fused_computation.10 | convolution fusion | flops 4831838208 | bytes 8126464 | tf_op jit(solution)/shard_map/dot_general | solution.py:8
  90.0 0.0 all-reduce.8.cloned.1.call-update
  90.0 0.6 copy-done.4
  90.7 0.6 dynamic-slice
  91.9 1.6 constant_dynamic-slice_fusion
  93.5 199.3 %all-reduce.8.cloned.1.call-done = (f32[512,2048]{1,0:T(8,128)}, f32[512,128]{1,0:T(8,128)}) async-done(((f32[512,2048]{1,0:T(8,128)}, f32[512,128]{1,0:T(8,128)}), (f32[512,2048]{1,0:T(8,128)}, f32[512,128]{1,0:T(8,128)})) %all-reduce.8.cloned.1.call-update) | async-done | bytes 4456464
  292.8 0.0 copy-done.3
  292.8 1.3 fusion.5
  294.1 0.0 copy-done.2
  294.1 1.5 dynamic-slice_subtract_fusion
  295.6 0.0 all-to-all-done
  295.6 9.6 %fusion.2 = f32[384,2048]{1,0:T(8,128)} fusion(f32[384,2048]{1,0:T(8,128)} %param.13, f32[384,512]{1,0:T(8,128)} %all-reduce.6.cloned.1.call-done, f32[64,8,2048]{2,1,0:T(8,128)} %all-to-all-done), kind=kOutput, calls=%fused_computation.2 | convolution fusion | flops 4832624640 | bytes 11272192 | tf_op jit(solution)/shard_map/dot_general | solution.py:27
  (5 shorter events, 0.0 us)
Async XLA Ops:
  7.2 73.4 %copy-start = (f32[384,2048]{1,0:T(8,128)S(1)}, f32[384,2048]{1,0:T(8,128)}, u32[]{:S(2)}) copy-start(f32[384,2048]{1,0:T(8,128)} %param.12) | copy-start | bytes 9437188
  10.7 13.5 %copy-start.1 = (f32[128,512]{1,0:T(8,128)S(1)}, f32[128,512]{1,0:T(8,128)}, u32[]{:S(2)}) copy-start(f32[128,512]{1,0:T(8,128)} %param.9) | copy-start | bytes 786436
  10.7 285.0 %all-to-all-start = ((f32[64,8,2048]{2,1,0:T(8,128)}), f32[64,8,2048]{2,1,0:T(8,128)}, u32[]{:S(2)}, u32[]{:S(2)}) async-start(f32[64,8,2048]{2,1,0:T(8,128)} %stack.2), calls=%async_computation | async-start | bytes 8388608 | tf_op jit(solution)/shard_map/all_to_all | solution.py:30
  24.1 53.1 %all-reduce.6.cloned.1.call-start = ((), (), s32[]{:S(2)}) async-start(), calls=%async_computation.1 | async-start | bytes 1572864 | tf_op jit(solution)/shard_map/psum | solution.py:25
  26.8 266.0 %all-reduce.8.cloned.1.call-start = ((), (), s32[]{:S(2)}) async-start(), calls=%async_computation.2 | async-start | bytes 8912896
  90.0 0.7 copy-start.4
  90.0 202.8 %copy-start.3 = (f32[8,128]{1,0:T(8,128)S(1)}, f32[8,128]{1,0:T(8,128)}, u32[]{:S(2)}) copy-start(f32[8,128]{1,0:T(8,128)} %param.15) | copy-start | bytes 12292
  90.0 204.2 %copy-start.2 = (f32[8,2048]{1,0:T(8,128)S(1)}, f32[8,2048]{1,0:T(8,128)}, u32[]{:S(2)}) copy-start(f32[8,2048]{1,0:T(8,128)} %param.14) | copy-start | bytes 196612
Sparse Core Ops, SparseCore 0:
  27.9 49.3 all-reduce.5
  90.1 202.6 all-reduce.7

commit v2 on v0

--- a/solution.py
+++ b/solution.py
@@ -22,7 +22,9 @@
     partial_panel = jnp.dot(
         panel_adj, inv_tile, precision=precise, preferred_element_type=jnp.float32
     )
-    scaled = lax.psum(partial_panel, "col")
+    scaled = partial_panel
+    for hop in (1, 2):
+        scaled = scaled + lax.ppermute(scaled, "col", [(dev, dev ^ hop) for dev in range(4)])
     panel_out = lax.dynamic_slice_in_dim(scaled, col_place * col_width, col_width, 1)
     slab_out = slab_adj - jnp.dot(
         scaled,

time: 371 us -> 358 us (0.965)
  waiting for transfers between devices: 327 us -> 309 us
  starting transfers between devices: 0.12 us -> 6.23 us
    psum x1 -> x0, waiting for transfers between devices: 52.2 us -> none  [per_device(): scaled = lax.psum(partial_panel, 'col')]
    ppermute x0 -> x2, waiting for transfers between devices: none -> 32.1 us  [per_device(): lax.ppermute(scaled, 'col', [(dev, dev ^ hop) for dev in range(4)])]
    ppermute x0 -> x2, starting transfers between devices: none -> 6.15 us  [per_device(): lax.ppermute(scaled, 'col', [(dev, dev ^ hop) for dev in range(4)])]
    unnamed x4 -> x3, waiting for transfers between devices: 195 us -> 197 us
  transfers between devices with their start and end apart: 3 -> 4, of which waited for: 3 -> 4; matrix products, arithmetic and copies ran while one was open for 1% -> 1% of each run, Pallas kernels for 0% -> 0%
where the time goes in v2:
time: 358 us
  waiting for transfers between devices  309 us (86%)
  matrix products  22.1 us (6%)
  between operations  14.8 us (4%)
  starting transfers between devices  6.23 us (2%)
    unnamed x3, waiting for transfers between devices  197 us
    all_gather x1, waiting for transfers between devices, per_device(): lax.all_gather(block_row, 'row', axis=0, tiled=True)  80.1 us
    ppermute x2, waiting for transfers between devices, per_device(): lax.ppermute(scaled, 'col', [(dev, dev ^ hop) for dev in range(4)])  32.1 us
    dot_general x2, matrix products, contract_rows(): lax.dot_general(left, right, (((0,), (0,)), ((), ())), precision=lax.Prec...  10.6 us
    dot_general x1, matrix products, per_device(): jnp.dot(scaled, lax.all_gather(block_row, 'row', axis=0, tiled=True), pre...  9.61 us
  transfers between devices with their start and end apart: 4, of which 4 were waited for; matrix products, arithmetic and copies ran while one was open for 1% of the time, Pallas kernels for 0%

profile of v2, /device:TPU:1, one launch (start us, length us, event | category | flops | bytes accessed | tf_op | source)
XLA Modules:
  0.0 357.8 jit_solution(14183771679890586457)
XLA Ops:
  7.2 0.0 copy-start
  7.2 0.0 all-reduce.5.cloned.1.call-start
  7.2 2.0 fusion.1
  9.2 2.1 collective-permute-start
  11.3 16.0 %collective-permute-done = f32[384,512]{1,0:T(8,128)S(1)} collective-permute-done((f32[384,512]{1,0:T(8,128)S(1)}, f32[384,512]{1,0:T(8,128)S(1)}, u32[]{:S(2)}, u32[]{:S(2)}) %collective-permute-start) | collective-permute-done | bytes 786464 | tf_op jit(solution)/shard_map/ppermute | solution.py:27
  27.3 0.1 add.27
  27.5 4.0 %collective-permute-start.1 = (f32[384,512]{1,0:T(8,128)S(1)}, f32[384,512]{1,0:T(8,128)S(1)}, u32[]{:S(2)}, u32[]{:S(2)}) collective-permute-start(f32[384,512]{1,0:T(8,128)S(1)} %add.27), channel_id=1, source_target_pairs={{0,2},{1,3},{2,0},{3,1},{4,6},{5,7},{6,4},{7,5},{8,10},{9,11},{10,... | collective-permute-start | bytes 2359304 | tf_op jit(solution)/shard_map/ppermute | solution.py:27
  31.5 16.1 %collective-permute-done.1 = f32[384,512]{1,0:T(8,128)S(1)} collective-permute-done((f32[384,512]{1,0:T(8,128)S(1)}, f32[384,512]{1,0:T(8,128)S(1)}, u32[]{:S(2)}, u32[]{:S(2)}) %collective-permute-start.1) | collective-permute-done | bytes 786464 | tf_op jit(solution)/shard_map/ppermute | solution.py:27
  47.6 0.1 add.28
  47.8 0.0 copy-done
  47.8 0.0 copy-start.2
  47.8 8.4 %fusion.2 = f32[512,2048]{1,0:T(8,128)} fusion(f32[384,512]{1,0:T(8,128)S(1)} %add.28, f32[384,2048]{1,0:T(8,128)S(1)} %copy-done), kind=kOutput, calls=%fused_computation.8 | convolution fusion | flops 4831838208 | bytes 8126464 | tf_op jit(solution)/shard_map/dot_general | solution.py:8
  56.2 0.0 copy-start.3
  56.2 2.2 fusion.3
  58.4 0.0 all-reduce.5.cloned.1.call-update
  58.4 0.0 all-gather.2.cloned.1.call-start
  58.5 0.7 all-gather.2.cloned.1.call-update
  59.2 0.6 dynamic-slice
  60.4 1.6 constant_dynamic-slice_fusion
  62.1 196.3 %all-reduce.5.cloned.1.call-done = (f32[512,2048]{1,0:T(8,128)}, f32[512,128]{1,0:T(8,128)}) async-done(((f32[512,2048]{1,0:T(8,128)}, f32[512,128]{1,0:T(8,128)}), (f32[512,2048]{1,0:T(8,128)}, f32[512,128]{1,0:T(8,128)})) %all-reduce.5.cloned.1.call-update) | async-done | bytes 4456464
  258.4 1.3 fusion
  259.8 1.5 dynamic-slice_subtract_fusion
  261.2 80.1 %all-gather.2.cloned.1.call-done = f32[512,2048]{1,0:T(8,128)} async-done(((f32[8,2048]{1,0:T(8,128)}), f32[512,2048]{1,0:T(8,128)}) %all-gather.2.cloned.1.call-update) | async-done | bytes 4194320 | tf_op jit(solution)/shard_map/all_gather | solution.py:31
  341.4 9.6 %convolution_subtract_fusion = f32[384,2048]{1,0:T(8,128)} fusion(f32[384,2048]{1,0:T(8,128)} %param.13, f32[384,512]{1,0:T(8,128)} %copy-done.1, f32[512,2048]{1,0:T(8,128)} %all-gather.2.cloned.1.call-done), kind=kOutput, calls=%fused_computation | convolution fusion | flops 4832624640 | bytes 11272192 | tf_op jit(solution)/shard_map/dot_general | solution.py:29
  (10 shorter events, 0.0 us)
Async XLA Ops:
  7.2 40.6 %copy-start = (f32[384,2048]{1,0:T(8,128)S(1)}, f32[384,2048]{1,0:T(8,128)}, u32[]{:S(2)}) copy-start(f32[384,2048]{1,0:T(8,128)} %param.12) | copy-start | bytes 9437188
  7.2 251.2 %all-reduce.5.cloned.1.call-start = ((), (), s32[]{:S(2)}) async-start(), calls=%async_computation.1 | async-start | bytes 8912896
  9.2 18.1 %collective-permute-start = (f32[384,512]{1,0:T(8,128)S(1)}, f32[384,512]{1,0:T(8,128)S(1)}, u32[]{:S(2)}, u32[]{:S(2)}) collective-permute-start(f32[384,512]{1,0:T(8,128)S(1)} %fusion.1), channel_id=1, source_target_pairs={{0,1},{1,0},{2,3},{3,2},{4,5},{5,4},{6,7},{7,6},{8,9},{9,8},{10,11... | collective-permute-start | bytes 2359304 | tf_op jit(solution)/shard_map/ppermute | solution.py:27
  27.5 20.2 %collective-permute-start.1 = (f32[384,512]{1,0:T(8,128)S(1)}, f32[384,512]{1,0:T(8,128)S(1)}, u32[]{:S(2)}, u32[]{:S(2)}) collective-permute-start(f32[384,512]{1,0:T(8,128)S(1)} %add.27), channel_id=1, source_target_pairs={{0,2},{1,3},{2,0},{3,1},{4,6},{5,7},{6,4},{7,5},{8,10},{9,11},{10,... | collective-permute-start | bytes 2359304 | tf_op jit(solution)/shard_map/ppermute | solution.py:27
  47.8 8.4 %copy-start.1 = (f32[384,512]{1,0:T(8,128)}, f32[384,512]{1,0:T(8,128)S(1)}, u32[]{:S(2)}) copy-start(f32[384,512]{1,0:T(8,128)S(1)} %add.28) | copy-start | bytes 2359300
  47.8 8.4 %copy-start.2 = (f32[384,128]{1,0:T(8,128)S(1)}, f32[384,128]{1,0:T(8,128)}, u32[]{:S(2)}) copy-start(f32[384,128]{1,0:T(8,128)} %param.10) | copy-start | bytes 589828
  56.2 3.0 copy-start.5
  56.2 202.2 %copy-start.4 = (f32[8,128]{1,0:T(8,128)S(1)}, f32[8,128]{1,0:T(8,128)}, u32[]{:S(2)}) copy-start(f32[8,128]{1,0:T(8,128)} %param.15) | copy-start | bytes 12292
  56.2 203.6 %copy-start.3 = (f32[8,2048]{1,0:T(8,128)S(1)}, f32[8,2048]{1,0:T(8,128)}, u32[]{:S(2)}) copy-start(f32[8,2048]{1,0:T(8,128)} %param.14) | copy-start | bytes 196612
  58.4 283.0 %all-gather.2.cloned.1.call-start = ((), (), s32[]{:S(2)}) async-start(), calls=%async_computation | async-start | bytes 4259840 | tf_op jit(solution)/shard_map/all_gather | solution.py:31
Sparse Core Ops, SparseCore 0:
  58.5 199.8 all-reduce.4
  261.2 80.1 all-gather.1
